TPU v7x, 128 devices: a whole 4x4x4 slice. The times are simulated.
128 devices in a mesh: rows: 8 (over y, z_lo), pairs: 16 (over z_hi, x, core).
Axes of the slice: x: 4, y: 4, z: 4 (z_hi: 2, z_lo: 2; z = z_hi * 2 + z_lo), core: 2. Of those that a mesh axis runs over, the one named last changes fastest.
Arguments:
- unit_rows: float32 [8, 16, 192, 8192], P('rows', 'pairs'), may hold values from -6 to 6
- unit_counts: int32 [8, 16], P('rows'), may hold values from 1 to 192, 1024 in all within a row
- seating: int32 [32], replicated, may hold values from 0 to 31, each once
- channel_scale: float32 [8192], replicated, may hold values from 0.25 to 4
Outputs:
- rotated: float32 [8192, 8192], P('rows', 'pairs')
Inputs may be any that keep to these rules, and one draw needn't show every extreme that they name: `unit_counts`: each row of 16 counts sums to 1024, and in each row the largest is exactly 192. `seating`: each block once.
All inputs are finite; a program needn't handle non-finite values.
Results may differ from a plain program's by a relative error of at most 0.0001.
Values sent between devices are 32-bit elements; how exact they have to be, the bound alone decides.
No kernel may reach another device: no remote copies, remote signals or barrier semaphores. Data moves between devices by JAX's collectives and lax.ppermute only.
A program may use at most 128 MiB of HBM per device.

v0:
```python
import jax
import jax.numpy as jnp
from jax import lax
from jax.sharding import PartitionSpec as P

ROWS_DEV = 1024
BLOCK = 256
ROUNDS = 2
epsilon = 1e-06


def passed_along(array, axis, by):
    length = lax.axis_size(axis)
    pairs = [(i, i + by) for i in range(length) if 0 <= i + by < length]
    return lax.ppermute(array, axis, pairs)


def rotate(panels):
    partial_gram = lax.dot_general(
        panels,
        panels,
        (((0,), (0,)), ((), ())),
        precision=lax.Precision.HIGHEST,
        preferred_element_type=jnp.float32,
    )
    gram_full = lax.psum(partial_gram, "rows")
    diag_terms = jnp.diagonal(gram_full)
    skew_part = (
        gram_full
        * (diag_terms[None, :] - diag_terms[:, None])
        / (2.0 * (diag_terms[:, None] ** 2 + diag_terms[None, :] ** 2) + epsilon)
    )
    skew_square = jnp.dot(skew_part, skew_part, precision=lax.Precision.HIGHEST)
    identity = jnp.eye(skew_part.shape[0], dtype=jnp.float32)
    numerator = identity + skew_part + 0.25 * skew_square
    sym_part = identity - 0.25 * skew_square
    factor = jnp.linalg.cholesky(sym_part)
    transposed = jax.scipy.linalg.cho_solve((factor, True), numerator.T)
    return jnp.dot(panels, transposed.T, precision=lax.Precision.HIGHEST)


def advance(panels):
    half_width = panels.shape[1] // 2
    upper = panels[:, :half_width]
    lower = panels[:, half_width:]
    pair_index = lax.axis_index("pairs")
    last_pair = lax.axis_size("pairs") - 1
    upward = jnp.where(pair_index == 0, lower, upper)
    came_up = passed_along(upward, "pairs", 1)
    came_down = passed_along(lower, "pairs", -1)
    new_upper = jnp.where(pair_index == 0, upper, came_up)
    new_lower = jnp.where(pair_index == last_pair, upper, came_down)
    return jnp.concatenate([new_upper, new_lower], axis=1)


def compact(panels, group_counts, capacity):
    unit_ends = jnp.cumsum(group_counts)
    target = lax.iota(jnp.int32, ROWS_DEV)
    passed = (target[:, None] >= unit_ends[None, :]).astype(jnp.int32)
    owner_unit = jnp.sum(passed, axis=1)
    owner_start = jnp.sum(passed * group_counts[None, :], axis=1)
    source = owner_unit * capacity + target - owner_start
    return jnp.take(panels, source, axis=0)


def local(unit_rows, unit_counts, seating, channel_scale):
    capacity = unit_rows.shape[2]
    columns = unit_rows.shape[3]
    group_counts = unit_counts[0]
    pair_index = lax.axis_index("pairs")
    slot_ids = lax.iota(jnp.int32, group_counts.shape[0])
    own_count = jnp.sum(jnp.where(slot_ids == pair_index, group_counts, 0))
    live_rows = (lax.iota(jnp.int32, capacity) < own_count)[:, None]
    scaled = jnp.where(live_rows, unit_rows[0, 0] * channel_scale[None, :], 0.0)
    seated = jnp.take(scaled.reshape(capacity, columns // BLOCK, BLOCK), seating, axis=1).reshape(
        capacity, columns
    )
    panels = lax.all_to_all(seated, "pairs", split_axis=1, concat_axis=0, tiled=True)
    current = panels
    for round_index in range(ROUNDS):
        current = rotate(current)
        if round_index + 1 < ROUNDS:
            current = advance(current)
    current = compact(current, group_counts, capacity)
    return current


def solution(mesh):
    return jax.shard_map(
        local,
        mesh=mesh,
        in_specs=(P("rows", "pairs", None, None), P("rows", None), P(), P()),
        out_specs=P("rows", "pairs"),
        check_vma=False,
    )
```

profile of v0, /device:TPU:2, one launch (start us, length us, event | category | flops | bytes accessed | tf_op | source)
XLA Modules:
  0.0 759.4 jit_solution(14425828180244923408)
XLA Ops:
  9.8 7.8 %copy.47 = f32[24,8,32,256]{3,2,1,0:T(8,128)} copy(f32[24,8,32,256]{3,1,2,0:T(8,128)} %bitcast.147) | data formatting | bytes 12582912
  17.7 9.5 %fusion.2 = f32[192,32,256]{2,0,1:T(8,128)} fusion(f32[192,32,256]{2,1,0:T(8,128)} %bitcast.144, f32[32,256]{1,0:T(8,128)S(1)} %mul.64, pred[192]{0:T(512)(128)(4,1)S(1)} %iota_compare_fusion.5), kind=kLoop, calls=%fused_computation.13 | loop fusion | flops 3145728 | bytes 12615872 | tf_op jit(solution)/shard_map/jit(_where)/select_n | solution.py:74
  27.2 6.4 gather_fusion
  33.6 9.1 %copy.33 = f32[192,32,256]{2,1,0:T(8,128)} copy(f32[192,32,256]{2,0,1:T(8,128)} %bitcast.145) | data formatting | bytes 12582912 | tf_op jit(solution)/shard_map/jit(_take)/gather | solution.py:75
  42.6 7.7 %gather.22 = f32[192,16,512]{2,1,0:T(8,128)} reshape(f32[192,32,256]{2,1,0:T(8,128)} %copy.33) | data formatting | bytes 12582912 | tf_op jit(solution)/shard_map/jit(_take)/gather | solution.py:75
  50.5 6.8 copy_select_fusion
  57.3 78.5 %all_to_all.16 = f32[192,16,512]{2,0,1:T(8,128)S(1)} all-to-all(f32[192,16,512]{2,0,1:T(8,128)S(1)} %copy_select_fusion), channel_id=1, replica_groups=mesh['rows'=8,'pairs'=16] {'pairs'}, dimensions={1} | all-to-all | bytes 12582912 | tf_op jit(solution)/shard_map/all_to_all | solution.py:78
  135.8 2.7 copy-done.1
  138.5 11.4 %fusion.5 = f32[512,512]{0,1:T(8,128)} fusion(f32[192,16,512]{2,0,1:T(8,128)S(1)} %all_to_all.16), kind=kOutput, calls=%fused_computation.23 | convolution fusion | flops 9663676416 | bytes 7340032 | tf_op jit(solution)/shard_map/dot_general | solution.py:19
  150.0 78.3 %all-reduce.4.cloned.1.call-done = f32[512,512]{0,1:T(8,128)} async-done(((f32[512,512]{0,1:T(8,128)}), f32[512,512]{0,1:T(8,128)}) %all-reduce.4.cloned.1.call-update) | async-done | bytes 1048592 | tf_op jit(solution)/shard_map/psum | solution.py:26
  228.3 9.0 %gather_fusion.1 = f32[512]{0:T(512)S(1)} fusion(f32[512,512]{0,1:T(8,128)} %all-reduce.4.cloned.1.call-done, s32[512]{0:T(512)S(1)} %bitcast.142), kind=kCustom, calls=%fused_computation.1 | custom fusion | bytes 8192 | tf_op jit(solution)/shard_map/jit(diagonal)/cond/branch_0_fun/gather | solution.py:27
  237.3 4.1 convolution_multiply_fusion.1
  241.4 1.4 convert_subtract_fusion.1
  244.4 11.7 %cholesky.286 = f32[128,128]{1,0:T(8,128)S(1)} custom-call(f32[128,128]{1,0:T(8,128)S(1)} %cholesky.426), custom_call_target="Cholesky" | custom-call | tf_op jit(solution)/shard_map/jit(cholesky)/cholesky | solution.py:37
  256.1 9.8 %custom-call.33 = f32[1,128,128]{1,2,0:T(8,128)S(1)} custom-call(f32[1,128,128]{2,1,0:T(8,128)S(1)} %get-tuple-element.72), custom_call_target="InvertDiagBlocksLowerTriangular" | custom-call | tf_op jit(solution)/shard_map/jit(cholesky)/cholesky | solution.py:37
  268.6 11.9 %cholesky.305 = f32[128,128]{1,0:T(8,128)S(1)} custom-call(f32[128,128]{1,0:T(8,128)S(1)} %cholesky.430), custom_call_target="Cholesky" | custom-call | tf_op jit(solution)/shard_map/jit(cholesky)/cholesky | solution.py:37
  280.5 9.8 %custom-call.34 = f32[1,128,128]{1,2,0:T(8,128)S(1)} custom-call(f32[1,128,128]{2,1,0:T(8,128)S(1)} %get-tuple-element.69), custom_call_target="InvertDiagBlocksLowerTriangular" | custom-call | tf_op jit(solution)/shard_map/jit(cholesky)/cholesky | solution.py:37
  291.9 11.7 %cholesky.326 = f32[128,128]{1,0:T(8,128)S(1)} custom-call(f32[128,128]{1,0:T(8,128)S(1)} %cholesky.435), custom_call_target="Cholesky" | custom-call | tf_op jit(solution)/shard_map/jit(cholesky)/cholesky | solution.py:37
  304.3 9.8 %custom-call.35 = f32[1,128,128]{1,2,0:T(8,128)S(1)} custom-call(f32[1,128,128]{2,1,0:T(8,128)S(1)} %get-tuple-element.66), custom_call_target="InvertDiagBlocksLowerTriangular" | custom-call | tf_op jit(solution)/shard_map/jit(cholesky)/cholesky | solution.py:37
  315.5 11.9 %cholesky.343 = f32[128,128]{1,0:T(8,128)S(1)} custom-call(f32[128,128]{1,0:T(8,128)S(1)} %convolution_subtract_fusion.17), custom_call_target="Cholesky" | custom-call | tf_op jit(solution)/shard_map/jit(cholesky)/cholesky | solution.py:37
  331.4 7.8 %while.4 = (s32[]{:T(128)}, f32[512,512]{1,0:T(8,128)S(1)}, s32[4,2]{0,1:T(2,128)S(1)}, f32[4,128,128]{2,1,0:T(8,128)S(1)}, s32[]{:T(128)}) while((s32[]{:T(128)}, f32[512,512]{1,0:T(8,128)S(1)}, s32[4,2]{0,1:T(2,128)S(1)}, f32[4,128,128]{2,1,0:T(8,128)S(1)}, s32[]{:T(128)}) %tuple.56), condition=%wide.while_cond, body=%wide.while_body.sunk | while | flops 2 | bytes 131181 | solution.py:38
  337.8 1.3 bitcast_dynamic-update-slice_fusion.4
  339.2 39.3 %custom-call.36 = f32[4,128,128]{1,2,0:T(8,128)S(1)} custom-call(f32[4,128,128]{2,1,0:T(8,128)S(1)} %get-tuple-element.21), custom_call_target="InvertDiagBlocksLowerTriangular" | custom-call | tf_op jit(solution)/shard_map/jit(_cho_solve)/triangular_solve | solution.py:38
  384.8 13.0 %fusion.12 = f32[3072,512]{0,1:T(8,128)S(1)} fusion(f32[3072,512]{1,0:T(8,128)} %bitcast.146, f32[128,512]{1,0:T(8,128)S(1)} %fusion.104, f32[128,512]{1,0:T(8,128)S(1)} %fusion.102, f32[128,512]{1,0:T(8,128)S(1)} %fusion.100, f32[128,512]{1,0:T(8,128)S(1)} %fusion.99), kind=kOutput, calls=%fused_computation.54 | convolution fusion | flops 9664462848 | bytes 13631488 | tf_op jit(solution)/shard_map/dot_general | solution.py:39
  397.8 2.5 slice_select_fusion.2
  401.4 1.9 collective-permute-start
  403.3 3.6 collective-permute-start.1
  407.0 33.3 %collective-permute-done = f32[3072,256]{0,1:T(8,128)} collective-permute-done((f32[3072,256]{0,1:T(8,128)}, f32[3072,256]{0,1:T(8,128)}, u32[]{:S(2)}, u32[]{:S(2)}) %collective-permute-start) | collective-permute-done | bytes 3145760 | tf_op jit(solution)/shard_map/ppermute | solution.py:15
  440.3 1.4 collective-permute-done.1
  441.7 4.5 slice_select_fusion.1
  446.3 1.6 copy-done.2
  448.0 11.7 %fusion.4 = f32[512,512]{0,1:T(8,128)} fusion(f32[3072,256]{0,1:T(8,128)S(1)} %get-tuple-element.46, f32[3072,256]{0,1:T(8,128)S(1)} %get-tuple-element.45), kind=kOutput, calls=%fused_computation.15 | convolution fusion | flops 9665249280 | bytes 7340032 | tf_op jit(solution)/shard_map/dot_general | solution.py:19
  460.1 81.0 %all-reduce.6.cloned.1.call-done = f32[512,512]{0,1:T(8,128)} async-done(((f32[512,512]{0,1:T(8,128)}), f32[512,512]{0,1:T(8,128)}) %all-reduce.6.cloned.1.call-update) | async-done | bytes 1048592 | tf_op jit(solution)/shard_map/psum | solution.py:26
  541.2 8.7 %gather_fusion.2 = f32[512]{0:T(512)S(1)} fusion(f32[512,512]{0,1:T(8,128)} %all-reduce.6.cloned.1.call-done, s32[512]{0:T(512)S(1)} %bitcast.143), kind=kCustom, calls=%fused_computation.2 | custom fusion | bytes 8192 | tf_op jit(solution)/shard_map/jit(diagonal)/cond/branch_0_fun/gather | solution.py:27
  549.9 4.0 convolution_multiply_fusion
  553.9 1.8 convert_subtract_fusion
  555.7 2.6 copy.40
  558.3 1.8 fusion.27
  561.0 11.7 %cholesky.358 = f32[128,128]{1,0:T(8,128)S(1)} custom-call(f32[128,128]{1,0:T(8,128)S(1)} %cholesky.439), custom_call_target="Cholesky" | custom-call | tf_op jit(solution)/shard_map/jit(cholesky)/cholesky | solution.py:37
  573.9 9.8 %custom-call.37 = f32[1,128,128]{1,2,0:T(8,128)S(1)} custom-call(f32[1,128,128]{2,1,0:T(8,128)S(1)} %get-tuple-element.62), custom_call_target="InvertDiagBlocksLowerTriangular" | custom-call | tf_op jit(solution)/shard_map/jit(cholesky)/cholesky | solution.py:37
  583.7 1.9 constant_dynamic-update-slice_fusion.3
  586.9 11.9 %cholesky.377 = f32[128,128]{1,0:T(8,128)S(1)} custom-call(f32[128,128]{1,0:T(8,128)S(1)} %cholesky.443), custom_call_target="Cholesky" | custom-call | tf_op jit(solution)/shard_map/jit(cholesky)/cholesky | solution.py:37
  600.8 9.8 %custom-call.38 = f32[1,128,128]{1,2,0:T(8,128)S(1)} custom-call(f32[1,128,128]{2,1,0:T(8,128)S(1)} %get-tuple-element.59), custom_call_target="InvertDiagBlocksLowerTriangular" | custom-call | tf_op jit(solution)/shard_map/jit(cholesky)/cholesky | solution.py:37
  611.5 1.4 convolution_subtract_fusion.14
  613.0 11.7 %cholesky.398 = f32[128,128]{1,0:T(8,128)S(1)} custom-call(f32[128,128]{1,0:T(8,128)S(1)} %cholesky.448), custom_call_target="Cholesky" | custom-call | tf_op jit(solution)/shard_map/jit(cholesky)/cholesky | solution.py:37
  626.0 9.8 %custom-call.39 = f32[1,128,128]{1,2,0:T(8,128)S(1)} custom-call(f32[1,128,128]{2,1,0:T(8,128)S(1)} %get-tuple-element.56), custom_call_target="InvertDiagBlocksLowerTriangular" | custom-call | tf_op jit(solution)/shard_map/jit(cholesky)/cholesky | solution.py:37
  636.7 1.4 convolution_subtract_fusion.16
  638.1 12.1 %cholesky.415 = f32[128,128]{1,0:T(8,128)S(1)} custom-call(f32[128,128]{1,0:T(8,128)S(1)} %convolution_subtract_fusion.16), custom_call_target="Cholesky" | custom-call | tf_op jit(solution)/shard_map/jit(cholesky)/cholesky | solution.py:37
  654.1 2.3 select_select_fusion
  656.4 11.4 %while.5 = (s32[]{:T(128)}, f32[512,512]{1,0:T(8,128)}, s32[4,2]{0,1:T(2,128)S(1)}, f32[4,128,128]{2,1,0:T(8,128)S(1)}, s32[]{:T(128)}) while((s32[]{:T(128)}, f32[512,512]{1,0:T(8,128)}, s32[4,2]{0,1:T(2,128)S(1)}, f32[4,128,128]{2,1,0:T(8,128)S(1)}, s32[]{:T(128)}) %tuple.66), condition=%wide.while_cond.clone, body=%wide.while_body.clone.sunk | while | flops 2 | bytes 131181 | solution.py:38
  657.1 2.2 bitcast_dynamic-update-slice_fusion.5
  659.9 2.2 bitcast_dynamic-update-slice_fusion.5
  662.8 2.2 bitcast_dynamic-update-slice_fusion.5
  665.6 2.2 bitcast_dynamic-update-slice_fusion.5
  668.5 40.1 %custom-call.40 = f32[4,128,128]{1,2,0:T(8,128)S(1)} custom-call(f32[4,128,128]{2,1,0:T(8,128)} %copy-done.10), custom_call_target="InvertDiagBlocksLowerTriangular" | custom-call | tf_op jit(solution)/shard_map/jit(_cho_solve)/triangular_solve | solution.py:38
  708.6 1.5 fusion.61
  710.2 1.4 convolution_subtract_fusion.3
  712.0 1.4 convolution_subtract_fusion.2
  713.9 1.7 convolution_subtract_fusion.9
  718.0 1.4 convolution_subtract_fusion
  719.7 1.6 convolution_subtract_fusion.8
  721.7 22.3 %fusion.3 = f32[3072,512]{1,0:T(8,128)} fusion(f32[3072,256]{0,1:T(8,128)S(1)} %copy-done.3, f32[3072,256]{0,1:T(8,128)S(1)} %get-tuple-element.45, f32[128,512]{1,0:T(8,128)S(1)} %fusion.111, f32[128,512]{1,0:T(8,128)S(1)} %fusion.109, f32[128,512]{1,0:T(8,128)S(1)} %fusion.107, f32[128,512]{1,0:T(8,128)S(1)} %fusion.106), kind=kOutput, calls=%fused_computation.14 | convolution fusion | flops 9666035712 | bytes 13631488 | tf_op jit(solution)/shard_map/dot_general | solution.py:39
  744.0 6.8 gather_fusion.3
  750.8 1.5 broadcast_select_fusion
  (128 shorter events, 44.0 us)
Async XLA Ops:
  6.5 221.8 %all-reduce.4.cloned.1.call-start = ((), (), s32[]{:S(2)}) async-start(), calls=%async_computation.1 | async-start | bytes 2097152 | tf_op jit(solution)/shard_map/psum | solution.py:26
  9.8 7.8 %copy-start.11 = (f32[8192]{0:T(1024)S(1)}, f32[8192]{0:T(1024)}, u32[]{:S(2)}) copy-start(f32[8192]{0:T(1024)} %param.10) | copy-start | bytes 98308
  135.8 2.7 copy-start.1
  150.0 391.2 %all-reduce.6.cloned.1.call-start = ((), (), s32[]{:S(2)}) async-start(), calls=%async_computation.2 | async-start | bytes 2097152 | tf_op jit(solution)/shard_map/psum | solution.py:26
  228.3 13.0 %copy-start.5 = (f32[512,512]{0,1:T(8,128)S(1)}, f32[512,512]{0,1:T(8,128)}, u32[]{:S(2)}) copy-start(f32[512,512]{0,1:T(8,128)} %all-reduce.4.cloned.1.call-done) | copy-start | bytes 3145732
  243.1 135.4 %copy-start.7 = (f32[512,512]{1,0:T(8,128)S(1)}, f32[512,512]{1,0:T(8,128)}, u32[]{:S(2)}) copy-start(f32[512,512]{1,0:T(8,128)} %get-tuple-element.52) | copy-start | bytes 3145732
  243.3 1.0 copy-start.9
  397.8 3.6 copy-start
  401.4 38.9 %collective-permute-start = (f32[3072,256]{0,1:T(8,128)}, f32[3072,256]{0,1:T(8,128)}, u32[]{:S(2)}, u32[]{:S(2)}) collective-permute-start(f32[3072,256]{0,1:T(8,128)} %get-tuple-element.47), channel_id=1, source_target_pairs={{0,1},{1,2},{2,3},{3,4},{4,5},{5,6},{6,7},{7,8},{8,9},{9,10},{10,1... | collective-permute-start | bytes 9437192 | tf_op jit(solution)/shard_map/ppermute | solution.py:15
  403.3 38.4 %collective-permute-start.1 = (f32[3072,256]{0,1:T(8,128)S(1)}, f32[3072,256]{0,1:T(8,128)}, u32[]{:S(2)}, u32[]{:S(2)}) collective-permute-start(f32[3072,256]{0,1:T(8,128)S(1)} %get-tuple-element.48), channel_id=1, source_target_pairs={{1,0},{2,1},{3,2},{4,3},{5,4},{6,5},{7,6},{8,7},{9,8},{10,9},{11,1... | collective-permute-start | bytes 9437192 | tf_op jit(solution)/shard_map/ppermute | solution.py:15
  446.3 1.7 copy-start.2
  446.3 13.4 %copy-start.12 = (s32[1,16]{1,0:T(1,128)S(1)}, s32[1,16]{1,0:T(1,128)}, u32[]{:S(2)}) copy-start(s32[1,16]{1,0:T(1,128)} %param.8) | copy-start | bytes 196
  549.9 4.0 copy-start.4
  553.9 1.8 copy-start.6
  560.0 1.0 copy-start.8
  667.8 0.7 copy-start.10
  708.6 13.1 %copy-start.3 = (f32[3072,256]{0,1:T(8,128)S(1)}, f32[3072,256]{0,1:T(8,128)}, u32[]{:S(2)}) copy-start(f32[3072,256]{0,1:T(8,128)} %copy-done.2) | copy-start | bytes 9437188
Sparse Core Ops, SparseCore 0:
  150.1 78.1 all-reduce.3
  459.8 81.2 all-reduce.5
where the time goes:
time: 769 us; the launch traced here: 759 us
  other arithmetic  276 us (36%)
  waiting for transfers between devices  194 us (25%)
  matrix products  98.8 us (13%)
  local copies, waits for them, and re-layouts  86.9 us (11%)
  blocking collectives  78.5 us (10%)
  between operations  19.4 us (3%)
    another operation x29, other arithmetic, rotate(): factor = jnp.linalg.cholesky(sym_part)  160 us
    psum x2, waiting for transfers between devices, rotate(): gram_full = lax.psum(partial_gram, 'rows')  159 us
    another operation x5, other arithmetic, rotate(): transposed = jax.scipy.linalg.cho_solve((factor, True), numerator.T)  81.9 us
    all_to_all x1, blocking collectives, local(): lax.all_to_all(seated, 'pairs', split_axis=1, concat_axis=0, tiled=True)  78.5 us
    dot_general x2, matrix products, rotate(): return jnp.dot(panels, transposed.T, precision=lax.Precision.HIGHEST)  35.3 us
    ppermute x2, waiting for transfers between devices, passed_along(): return lax.ppermute(array, axis, pairs)  34.8 us
    dot_general x2, matrix products, rotate(): lax.dot_general(panels, panels, (((0,), (0,)), ((), ())), precision=lax.P...  23.2 us
    gather x3, local copies, waits for them, and re-layouts, local(): jnp.take(scaled.reshape(capacity, columns // BLOCK, BLOCK), seating, axis=1)  23.1 us
  transfers between devices with their start and end apart: 4, of which 4 were waited for; matrix products, arithmetic and copies ran while one was open for 0% of the time, Pallas kernels for 0%

commit v1 on v0

--- a/solution.py
+++ b/solution.py
@@ -23,7 +23,7 @@
         precision=lax.Precision.HIGHEST,
         preferred_element_type=jnp.float32,
     )
-    gram_full = lax.psum(partial_gram, "rows")
+    gram_full = jnp.sum(lax.all_gather(partial_gram, "rows"), axis=0)
     diag_terms = jnp.diagonal(gram_full)
     skew_part = (
         gram_full

time: 769 us -> 958 us (1.25)
  waiting for transfers between devices: 194 us -> 381 us
    all_gather x0 -> x2, waiting for transfers between devices: none -> 346 us  [rotate(): gram_full = jnp.sum(lax.all_gather(partial_gram, 'rows'), axis=0)]
    psum x2 -> x0, waiting for transfers between devices: 159 us -> none  [rotate(): gram_full = lax.psum(partial_gram, 'rows')]
where the time goes in v1:
time: 958 us; the launch traced here: 944 us
  waiting for transfers between devices  381 us (40%)
  other arithmetic  282 us (29%)
  matrix products  91 us (9%)
  local copies, waits for them, and re-layouts  85.6 us (9%)
  blocking collectives  78.5 us (8%)
  between operations  20 us (2%)
    all_gather x2, waiting for transfers between devices, rotate(): gram_full = jnp.sum(lax.all_gather(partial_gram, 'rows'), axis=0)  346 us
    another operation x29, other arithmetic, rotate(): factor = jnp.linalg.cholesky(sym_part)  159 us
    another operation x5, other arithmetic, rotate(): transposed = jax.scipy.linalg.cho_solve((factor, True), numerator.T)  80.7 us
    all_to_all x1, blocking collectives, local(): lax.all_to_all(seated, 'pairs', split_axis=1, concat_axis=0, tiled=True)  78.5 us
    ppermute x2, waiting for transfers between devices, passed_along(): return lax.ppermute(array, axis, pairs)  34.8 us
    dot_general x2, matrix products, rotate(): return jnp.dot(panels, transposed.T, precision=lax.Precision.HIGHEST)  34.7 us
    gather x3, local copies, waits for them, and re-layouts, local(): jnp.take(scaled.reshape(capacity, columns // BLOCK, BLOCK), seating, axis=1)  23.2 us
    dot_general x2, matrix products, rotate(): lax.dot_general(panels, panels, (((0,), (0,)), ((), ())), precision=lax.P...  23 us
  transfers between devices with their start and end apart: 4, of which 4 were waited for; matrix products, arithmetic and copies ran while one was open for 0% of the time, Pallas kernels for 0%

profile of v1, /device:TPU:2, one launch (start us, length us, event | category | flops | bytes accessed | tf_op | source)
XLA Modules:
  0.0 944.0 jit_solution(15105490155023903462)
XLA Ops:
  7.9 1.3 fusion.130
  9.8 7.8 copy.65
  17.7 9.5 %fusion.2 = f32[192,32,256]{2,0,1:T(8,128)} fusion(f32[192,32,256]{2,1,0:T(8,128)} %bitcast.153, f32[32,256]{1,0:T(8,128)S(1)} %mul.80, pred[192]{0:T(512)(128)(4,1)S(1)} %iota_compare_fusion.6), kind=kLoop, calls=%fused_computation.13 | loop fusion | flops 3145728 | bytes 12615872 | tf_op jit(solution)/shard_map/jit(_where)/select_n | solution.py:74
  27.2 6.4 gather_fusion
  33.6 9.1 copy.54
  42.6 7.7 gather.22
  50.6 6.8 copy_select_fusion
  57.4 78.5 %all_to_all.16 = f32[192,16,512]{2,0,1:T(8,128)S(1)} all-to-all(f32[192,16,512]{2,0,1:T(8,128)S(1)} %copy_select_fusion), channel_id=1, replica_groups=mesh['rows'=8,'pairs'=16] {'pairs'}, dimensions={1} | all-to-all | bytes 12582912 | tf_op jit(solution)/shard_map/all_to_all | solution.py:78
  135.9 2.7 copy-done.1
  138.6 11.4 %fusion.5 = f32[512,512]{1,0:T(8,128)} fusion(f32[192,16,512]{2,0,1:T(8,128)S(1)} %all_to_all.16), kind=kOutput, calls=%fused_computation.23 | convolution fusion | flops 9663676416 | bytes 7340032 | tf_op jit(solution)/shard_map/dot_general | solution.py:19
  150.1 168.7 %all-gather.5.cloned.1.call-done = f32[4096,512]{1,0:T(8,128)} async-done(((f32[512,512]{1,0:T(8,128)}), f32[4096,512]{1,0:T(8,128)}) %all-gather.5.cloned.1.call-update) | async-done | bytes 8388624 | tf_op jit(solution)/shard_map/all_gather | solution.py:26
  318.8 4.5 reduce_sum.54
  323.3 13.3 %gather_fusion.1 = f32[512]{0:T(512)S(1)} fusion(f32[512,512]{1,0:T(8,128)S(1)} %reduce_sum.54, s32[512]{0:T(512)S(1)} %bitcast.151), kind=kCustom, calls=%fused_computation.1 | custom fusion | bytes 8192 | tf_op jit(solution)/shard_map/jit(diagonal)/cond/branch_0_fun/gather | solution.py:27
  336.6 3.5 convert_subtract_fusion.1
  340.8 2.7 fusion.27
  343.5 11.7 %cholesky.286 = f32[128,128]{1,0:T(8,128)S(1)} custom-call(f32[128,128]{1,0:T(8,128)S(1)} %cholesky.426), custom_call_target="Cholesky" | custom-call | tf_op jit(solution)/shard_map/jit(cholesky)/cholesky | solution.py:37
  355.2 9.8 %custom-call.33 = f32[1,128,128]{1,2,0:T(8,128)S(1)} custom-call(f32[1,128,128]{2,1,0:T(8,128)S(1)} %get-tuple-element.72), custom_call_target="InvertDiagBlocksLowerTriangular" | custom-call | tf_op jit(solution)/shard_map/jit(cholesky)/cholesky | solution.py:37
  367.7 11.9 %cholesky.305 = f32[128,128]{1,0:T(8,128)S(1)} custom-call(f32[128,128]{1,0:T(8,128)S(1)} %cholesky.430), custom_call_target="Cholesky" | custom-call | tf_op jit(solution)/shard_map/jit(cholesky)/cholesky | solution.py:37
  379.6 9.8 %custom-call.34 = f32[1,128,128]{1,2,0:T(8,128)S(1)} custom-call(f32[1,128,128]{2,1,0:T(8,128)S(1)} %get-tuple-element.69), custom_call_target="InvertDiagBlocksLowerTriangular" | custom-call | tf_op jit(solution)/shard_map/jit(cholesky)/cholesky | solution.py:37
  391.0 11.7 %cholesky.326 = f32[128,128]{1,0:T(8,128)S(1)} custom-call(f32[128,128]{1,0:T(8,128)S(1)} %cholesky.435), custom_call_target="Cholesky" | custom-call | tf_op jit(solution)/shard_map/jit(cholesky)/cholesky | solution.py:37
  403.5 9.8 %custom-call.35 = f32[1,128,128]{1,2,0:T(8,128)S(1)} custom-call(f32[1,128,128]{2,1,0:T(8,128)S(1)} %get-tuple-element.66), custom_call_target="InvertDiagBlocksLowerTriangular" | custom-call | tf_op jit(solution)/shard_map/jit(cholesky)/cholesky | solution.py:37
  414.8 12.1 %cholesky.343 = f32[128,128]{1,0:T(8,128)S(1)} custom-call(f32[128,128]{1,0:T(8,128)S(1)} %convolution_subtract_fusion.17), custom_call_target="Cholesky" | custom-call | tf_op jit(solution)/shard_map/jit(cholesky)/cholesky | solution.py:37
  431.1 8.4 while.4
  431.8 1.4 bitcast_dynamic-update-slice_fusion.4
  433.9 1.4 bitcast_dynamic-update-slice_fusion.4
  436.0 1.4 bitcast_dynamic-update-slice_fusion.4
  438.1 1.4 bitcast_dynamic-update-slice_fusion.4
  439.5 39.3 %custom-call.36 = f32[4,128,128]{1,2,0:T(8,128)S(1)} custom-call(f32[4,128,128]{2,1,0:T(8,128)S(1)} %get-tuple-element.21), custom_call_target="InvertDiagBlocksLowerTriangular" | custom-call | tf_op jit(solution)/shard_map/jit(_cho_solve)/triangular_solve | solution.py:38
  485.1 12.8 %fusion.10 = f32[3072,512]{0,1:T(8,128)S(1)} fusion(f32[3072,512]{1,0:T(8,128)} %bitcast.155, f32[128,512]{1,0:T(8,128)S(1)} %fusion.121, f32[128,512]{1,0:T(8,128)S(1)} %fusion.119, f32[128,512]{1,0:T(8,128)S(1)} %fusion.117, f32[128,512]{1,0:T(8,128)S(1)} %fusion.116), kind=kOutput, calls=%fused_computation.52 | convolution fusion | flops 9664462848 | bytes 13631488 | tf_op jit(solution)/shard_map/dot_general | solution.py:39
  498.0 2.5 slice_select_fusion.2
  501.6 1.9 collective-permute-start
  503.5 3.6 collective-permute-start.1
  507.1 33.3 %collective-permute-done = f32[3072,256]{0,1:T(8,128)} collective-permute-done((f32[3072,256]{0,1:T(8,128)}, f32[3072,256]{0,1:T(8,128)}, u32[]{:S(2)}, u32[]{:S(2)}) %collective-permute-start) | collective-permute-done | bytes 3145760 | tf_op jit(solution)/shard_map/ppermute | solution.py:15
  540.5 1.4 collective-permute-done.1
  541.9 4.5 slice_select_fusion.1
  546.5 1.7 copy-done.2
  549.1 11.6 %fusion.4 = f32[512,512]{1,0:T(8,128)} fusion(f32[3072,256]{0,1:T(8,128)S(1)} %get-tuple-element.46, f32[3072,256]{0,1:T(8,128)S(1)} %get-tuple-element.45), kind=kOutput, calls=%fused_computation.15 | convolution fusion | flops 9665249280 | bytes 7340032 | tf_op jit(solution)/shard_map/dot_general | solution.py:19
  561.2 177.4 %all-gather.7.cloned.1.call-done = f32[4096,512]{1,0:T(8,128)} async-done(((f32[512,512]{1,0:T(8,128)}), f32[4096,512]{1,0:T(8,128)}) %all-gather.7.cloned.1.call-update) | async-done | bytes 8388624 | tf_op jit(solution)/shard_map/all_gather | solution.py:26
  738.5 4.5 reduce_sum.56
  743.1 4.9 gather_fusion.2
  748.3 3.5 convert_subtract_fusion
  752.1 2.7 fusion.26
  754.8 11.7 %cholesky.358 = f32[128,128]{1,0:T(8,128)S(1)} custom-call(f32[128,128]{1,0:T(8,128)S(1)} %cholesky.439), custom_call_target="Cholesky" | custom-call | tf_op jit(solution)/shard_map/jit(cholesky)/cholesky | solution.py:37
  766.7 9.8 %custom-call.37 = f32[1,128,128]{1,2,0:T(8,128)S(1)} custom-call(f32[1,128,128]{2,1,0:T(8,128)S(1)} %get-tuple-element.62), custom_call_target="InvertDiagBlocksLowerTriangular" | custom-call | tf_op jit(solution)/shard_map/jit(cholesky)/cholesky | solution.py:37
  777.2 11.9 %cholesky.377 = f32[128,128]{1,0:T(8,128)S(1)} custom-call(f32[128,128]{1,0:T(8,128)S(1)} %cholesky.443), custom_call_target="Cholesky" | custom-call | tf_op jit(solution)/shard_map/jit(cholesky)/cholesky | solution.py:37
  790.5 9.8 %custom-call.38 = f32[1,128,128]{1,2,0:T(8,128)S(1)} custom-call(f32[1,128,128]{2,1,0:T(8,128)S(1)} %get-tuple-element.59), custom_call_target="InvertDiagBlocksLowerTriangular" | custom-call | tf_op jit(solution)/shard_map/jit(cholesky)/cholesky | solution.py:37
  801.0 11.7 %cholesky.398 = f32[128,128]{1,0:T(8,128)S(1)} custom-call(f32[128,128]{1,0:T(8,128)S(1)} %cholesky.448), custom_call_target="Cholesky" | custom-call | tf_op jit(solution)/shard_map/jit(cholesky)/cholesky | solution.py:37
  813.4 9.8 %custom-call.39 = f32[1,128,128]{1,2,0:T(8,128)S(1)} custom-call(f32[1,128,128]{2,1,0:T(8,128)S(1)} %get-tuple-element.56), custom_call_target="InvertDiagBlocksLowerTriangular" | custom-call | tf_op jit(solution)/shard_map/jit(cholesky)/cholesky | solution.py:37
  823.8 11.9 %cholesky.415 = f32[128,128]{1,0:T(8,128)S(1)} custom-call(f32[128,128]{1,0:T(8,128)S(1)} %convolution_subtract_fusion.16), custom_call_target="Cholesky" | custom-call | tf_op jit(solution)/shard_map/jit(cholesky)/cholesky | solution.py:37
  840.3 12.3 %while.5 = (s32[]{:T(128)}, f32[512,512]{1,0:T(8,128)}, s32[4,2]{0,1:T(2,128)S(1)}, f32[4,128,128]{2,1,0:T(8,128)S(1)}, s32[]{:T(128)}) while((s32[]{:T(128)}, f32[512,512]{1,0:T(8,128)}, s32[4,2]{0,1:T(2,128)S(1)}, f32[4,128,128]{2,1,0:T(8,128)S(1)}, s32[]{:T(128)}) %tuple.68), condition=%wide.while_cond.clone, body=%wide.while_body.clone.sunk | while | flops 2 | bytes 131181 | solution.py:38
  841.0 2.6 bitcast_dynamic-update-slice_fusion.5
  844.2 2.3 bitcast_dynamic-update-slice_fusion.5
  847.2 2.3 bitcast_dynamic-update-slice_fusion.5
  850.3 2.3 bitcast_dynamic-update-slice_fusion.5
  853.3 40.1 %custom-call.40 = f32[4,128,128]{1,2,0:T(8,128)S(1)} custom-call(f32[4,128,128]{2,1,0:T(8,128)} %copy-done.8), custom_call_target="InvertDiagBlocksLowerTriangular" | custom-call | tf_op jit(solution)/shard_map/jit(_cho_solve)/triangular_solve | solution.py:38
  893.4 1.5 fusion.78
  894.9 1.4 convolution_subtract_fusion.3
  896.7 1.4 convolution_subtract_fusion.2
  898.6 1.7 convolution_subtract_fusion.9
  902.7 1.4 convolution_subtract_fusion
  904.5 1.6 convolution_subtract_fusion.8
  906.5 21.9 %fusion.3 = f32[3072,512]{1,0:T(8,128)} fusion(f32[3072,256]{0,1:T(8,128)S(1)} %copy-done.5, f32[3072,256]{0,1:T(8,128)S(1)} %copy-done.3, f32[128,512]{1,0:T(8,128)S(1)} %fusion.128, f32[128,512]{1,0:T(8,128)S(1)} %fusion.126, f32[128,512]{1,0:T(8,128)S(1)} %fusion.124, f32[128,512]{1,0:T(8,128)S(1)} %fusion.123), kind=kOutput, calls=%fused_computation.14 | convolution fusion | flops 9666035712 | bytes 13631488 | tf_op jit(solution)/shard_map/dot_general | solution.py:39
  928.3 6.8 gather_fusion.3
  935.1 1.5 broadcast_select_fusion
  (126 shorter events, 36.3 us)
Async XLA Ops:
  6.5 312.3 %all-gather.5.cloned.1.call-start = ((), (), s32[]{:S(2)}) async-start(), calls=%async_computation.1 | async-start | bytes 9437184 | tf_op jit(solution)/shard_map/all_gather | solution.py:26
  9.8 7.8 copy-start.9
  135.9 2.7 copy-start.1
  150.0 588.5 %all-gather.7.cloned.1.call-start = ((), (), s32[]{:S(2)}) async-start(), calls=%async_computation.2 | async-start | bytes 9437184 | tf_op jit(solution)/shard_map/all_gather | solution.py:26
  343.4 11.8 %copy-start.7 = (f32[512,512]{1,0:T(8,128)}, f32[512,512]{1,0:T(8,128)S(1)}, u32[]{:S(2)}) copy-start(f32[512,512]{1,0:T(8,128)S(1)} %get-tuple-element.51) | copy-start | bytes 3145732
  343.4 135.4 %copy-start.6 = (f32[512,512]{1,0:T(8,128)S(1)}, f32[512,512]{1,0:T(8,128)}, u32[]{:S(2)}) copy-start(f32[512,512]{1,0:T(8,128)} %get-tuple-element.52) | copy-start | bytes 3145732
  498.0 3.6 copy-start
  501.6 38.9 %collective-permute-start = (f32[3072,256]{0,1:T(8,128)}, f32[3072,256]{0,1:T(8,128)}, u32[]{:S(2)}, u32[]{:S(2)}) collective-permute-start(f32[3072,256]{0,1:T(8,128)} %get-tuple-element.47), channel_id=1, source_target_pairs={{0,1},{1,2},{2,3},{3,4},{4,5},{5,6},{6,7},{7,8},{8,9},{9,10},{10,1... | collective-permute-start | bytes 9437192 | tf_op jit(solution)/shard_map/ppermute | solution.py:15
  503.5 38.4 %collective-permute-start.1 = (f32[3072,256]{0,1:T(8,128)S(1)}, f32[3072,256]{0,1:T(8,128)}, u32[]{:S(2)}, u32[]{:S(2)}) collective-permute-start(f32[3072,256]{0,1:T(8,128)S(1)} %get-tuple-element.48), channel_id=1, source_target_pairs={{1,0},{2,1},{3,2},{4,3},{5,4},{6,5},{7,6},{8,7},{9,8},{10,9},{11,1... | collective-permute-start | bytes 9437192 | tf_op jit(solution)/shard_map/ppermute | solution.py:15
  546.5 1.7 copy-start.2
  546.5 2.7 copy-start.4
  546.5 14.3 %copy-start.10 = (s32[1,16]{1,0:T(1,128)S(1)}, s32[1,16]{1,0:T(1,128)}, u32[]{:S(2)}) copy-start(s32[1,16]{1,0:T(1,128)} %param.8) | copy-start | bytes 196
  840.3 66.2 %copy-start.3 = (f32[3072,256]{0,1:T(8,128)S(1)}, f32[3072,256]{0,1:T(8,128)}, u32[]{:S(2)}) copy-start(f32[3072,256]{0,1:T(8,128)} %copy-done.2) | copy-start | bytes 9437188
  852.5 0.7 copy-start.8
  893.4 13.1 %copy-start.5 = (f32[3072,256]{0,1:T(8,128)S(1)}, f32[3072,256]{0,1:T(8,128)}, u32[]{:S(2)}) copy-start(f32[3072,256]{0,1:T(8,128)} %copy-done.4) | copy-start | bytes 9437188
Sparse Core Ops, SparseCore 0:
  150.2 168.5 all-gather.4
  560.9 177.6 all-gather.6
